TPU v7x, 512 devices: a whole 4x8x8 slice. The times are simulated.
512 devices in a mesh: blk: 64 (over y, z), mpo: 8 (over x, core).
Axes of the slice: x: 4, y: 8, z: 8, core: 2. Of those that a mesh axis runs over, the one named last changes fastest.
Arguments:
- wave: bfloat16 [6144, 128, 128], P('blk'), may hold values from -6 to 6
- left_env: bfloat16 [8, 64, 128, 128], P('mpo', 'blk'), may hold values from -0.5 to 0.5
- right_env: bfloat16 [8, 64, 128, 128], P('mpo', 'blk'), may hold values from -0.1875 to 0.1875
- right_sector: int32 [6144, 1], P('blk'), may hold values from 0 to 63; in each aligned block of 96 rows (0 to 95, 96 to 191, ...) at most 2 rows name the same one
- right_home: int32 [64], replicated, may hold values from 0 to 63, each once
Outputs:
- product: bfloat16 [6144, 128, 128], P('blk', None, 'mpo')
Inputs may be any that keep to these rules, and one draw needn't show every extreme that they name: `right_sector`: among the 96 blocks of one device (aligned blocks of rows) no right sector appears more than 2 times, and some sector appears exactly 2 times; every sector appears somewhere. `right_home`: each sector has its own storage row.
All inputs are finite; a program needn't handle non-finite values.
Results may differ from a plain program's by a relative error of at most 0.008.
Values may be sent and summed in bfloat16 or wider, within the bound.
No kernel may reach another device: no remote copies, remote signals or barrier semaphores. Data moves between devices by JAX's collectives and lax.ppermute only.
A program may use at most 64 MiB of HBM per device.

v0:
```python
import jax
import jax.numpy as jnp
from jax import lax
from jax.sharding import PartitionSpec as P


def local(wave, left_env, right_env, right_sector, right_home):
    blocks = wave.shape[0]
    sectors = left_env.shape[1]
    local_left = jnp.arange(blocks, dtype=jnp.int32) * sectors // blocks
    places = jnp.take(right_home, right_sector[:, 0], axis=0)
    chosen = jnp.take(left_env[0], local_left, axis=0)
    left = jnp.einsum("bik,bkj->bij", chosen, wave, preferred_element_type=jnp.float32).astype(
        jnp.bfloat16
    )
    every_right = lax.all_gather(right_env[0], "blk", axis=0, tiled=True)
    picked = jnp.take(every_right, places, axis=0)
    terms = jnp.einsum("bik,bjk->bij", left, picked, preferred_element_type=jnp.float32)
    summed = lax.psum_scatter(terms, "mpo", scatter_dimension=2, tiled=True)
    return summed.astype(jnp.bfloat16)


def solution(mesh):
    in_specs = (
        P("blk", None, None),
        P("mpo", "blk", None, None),
        P("mpo", "blk", None, None),
        P("blk", None),
        P(),
    )
    out_specs = P("blk", None, "mpo")
    return jax.shard_map(local, mesh=mesh, in_specs=in_specs, out_specs=out_specs, check_vma=False)
```

profile of v0, /device:TPU:1, one launch (start us, length us, event | category | flops | bytes accessed | tf_op | source)
XLA Modules:
  0.0 164.5 jit_solution(18109808292682006214)
XLA Ops:
  6.5 0.0 copy-start
  6.5 0.0 all-gather.3.cloned.1.call-start
  6.5 0.7 all-gather.3.cloned.1.call-update
  7.3 0.0 reduce-scatter.2.cloned.1.call-start
  7.3 0.8 fusion.17
  8.1 1.6 gather_fusion
  9.7 0.7 and_bitcast_fusion
  10.4 84.6 %all-gather.3.cloned.1.call-done = bf16[64,1,128,128]{3,2,1,0:T(8,128)(2,1)} async-done(((bf16[1,1,128,128]{3,2,1,0:T(8,128)(2,1)}), bf16[64,1,128,128]{3,2,1,0:T(8,128)(2,1)}) %all-gather.3.cloned.1.call-update) | async-done | bytes 2097168 | tf_op jit(solution)/shard_map/all_gather | solution.py:16
  95.0 0.0 copy-start.1
  95.0 4.3 %gather_fusion.1 = bf16[96,128,128]{2,1,0:T(8,128)(2,1)} fusion(bf16[64,128,128]{2,1,0:T(8,128)(2,1)} %bitcast.13, s32[1024]{0:T(1024)S(1)} %pad_clamp_fusion), kind=kCustom, calls=%fused_computation.1 | custom fusion | bytes 6291840 | tf_op jit(solution)/shard_map/jit(_take)/gather | solution.py:17
  99.4 0.0 copy-done
  99.4 0.0 copy-done.1
  99.4 7.8 %fusion = f32[96,128,128]{1,2,0:T(8,128)} fusion(bf16[96,128,128]{2,1,0:T(8,128)(2,1)} %gather_fusion.1, pred[96]{0:T(512)(128)(4,1)S(1)} %get-tuple-element.5, bf16[96,128,128]{2,1,0:T(8,128)(2,1)S(1)} %copy-done, pred[96]{0:T(512)(128)(4,1)S(1)} %compare_and_fusion, bf16[128,128]{1,0:T(8,128)(2,1)S(1)} %bitcast.15), kind=kOutput, calls=%fused_computation.2 | convolution fusion | flops 810024960 | bytes 12615872 | tf_op jit(solution)/shard_map/bik,bjk->bij/dot_general | solution.py:18
  107.2 0.0 reduce-scatter.2.cloned.1.call-update
  107.2 48.5 %reduce-scatter.2.cloned.1.call-done = f32[96,128,16]{1,2,0:T(8,128)} async-done(((f32[96,128,128]{1,2,0:T(8,128)}), f32[96,128,16]{1,2,0:T(8,128)}) %reduce-scatter.2.cloned.1.call-update) | async-done | bytes 786448 | tf_op jit(solution)/shard_map/reduce_scatter | solution.py:19
  155.7 1.9 %convert_element_type.7 = bf16[96,128,16]{1,2,0:T(8,128)(2,1)} convert(f32[96,128,16]{1,2,0:T(8,128)} %reduce-scatter.2.cloned.1.call-done) | non-fusion elementwise | flops 196608 | bytes 1179648 | tf_op jit(solution)/shard_map/convert_element_type | solution.py:20
  (3 shorter events, 0.0 us)
Async XLA Ops:
  6.5 92.9 %copy-start = (bf16[96,128,128]{2,1,0:T(8,128)(2,1)S(1)}, bf16[96,128,128]{2,1,0:T(8,128)(2,1)}, u32[]{:S(2)}) copy-start(bf16[96,128,128]{2,1,0:T(8,128)(2,1)} %param.5) | copy-start | bytes 9437188
  6.5 88.5 %all-gather.3.cloned.1.call-start = ((), (), s32[]{:S(2)}) async-start(), calls=%async_computation.2 | async-start | bytes 2129920 | tf_op jit(solution)/shard_map/all_gather | solution.py:16
  7.3 148.5 %reduce-scatter.2.cloned.1.call-start = ((), (), s32[]{:S(2)}) async-start(), calls=%async_computation.1 | async-start | bytes 7077888 | tf_op jit(solution)/shard_map/reduce_scatter | solution.py:19
  95.0 4.4 %copy-start.1 = (bf16[1,1,128,128]{3,2,1,0:T(8,128)(2,1)S(1)}, bf16[1,1,128,128]{3,2,1,0:T(8,128)(2,1)}, u32[]{:S(2)}) copy-start(bf16[1,1,128,128]{3,2,1,0:T(8,128)(2,1)} %param.6) | copy-start | bytes 98308
Sparse Core Ops, SparseCore 0:
  10.3 84.6 all-gather.2
  107.3 48.3 reduce-scatter.1
where the time goes:
time: 165 us
  waiting for transfers between devices  134 us (81%)
  between operations  13.4 us (8%)
  matrix products  7.78 us (5%)
  local copies, waits for them, and re-layouts  5.94 us (4%)
  other arithmetic  3.45 us (2%)
    all_gather x1, waiting for transfers between devices, local(): every_right = lax.all_gather(right_env[0], 'blk', axis=0, tiled=True)  84.6 us
    reduce_scatter x1, waiting for transfers between devices, local(): summed = lax.psum_scatter(terms, 'mpo', scatter_dimension=2, tiled=True)  48.5 us
    dot_general x1, matrix products, local(): jnp.einsum('bik,bjk->bij', left, picked, preferred_element_type=jnp.float32)  7.78 us
    gather x1, local copies, waits for them, and re-layouts, local(): picked = jnp.take(every_right, places, axis=0)  4.35 us
  transfers between devices with their start and end apart: 2, of which 2 were waited for; matrix products, arithmetic and copies ran while one was open for 2% of the time, Pallas kernels for 0%

commit v1 on v0

--- a/solution.py
+++ b/solution.py
@@ -5,6 +5,13 @@
 
 
 def local(wave, left_env, right_env, right_sector, right_home):
+
+    def resolve_state(sample, peer_axis, d0):
+        reached = jnp.stack([sample] * lax.psum(1, peer_axis))
+        value_now = lax.all_to_all(reached, peer_axis, 0, 0)
+        x_new = jnp.concatenate(value_now, axis=d0)
+        return x_new
+
     blocks = wave.shape[0]
     sectors = left_env.shape[1]
     local_left = jnp.arange(blocks, dtype=jnp.int32) * sectors // blocks
@@ -13,7 +20,7 @@
     left = jnp.einsum("bik,bkj->bij", chosen, wave, preferred_element_type=jnp.float32).astype(
         jnp.bfloat16
     )
-    every_right = lax.all_gather(right_env[0], "blk", axis=0, tiled=True)
+    every_right = resolve_state(right_env[0], "blk", 0)
     picked = jnp.take(every_right, places, axis=0)
     terms = jnp.einsum("bik,bjk->bij", left, picked, preferred_element_type=jnp.float32)
     summed = lax.psum_scatter(terms, "mpo", scatter_dimension=2, tiled=True)

time: 165 us -> 147 us (0.89)
  waiting for transfers between devices: 134 us -> 97.8 us
  starting transfers between devices: 0.04 us -> 17.4 us
  local copies, waits for them, and re-layouts: 5.94 us -> 8.31 us
    all_gather x1 -> x0, waiting for transfers between devices: 84.6 us -> none  [local(): every_right = lax.all_gather(right_env[0], 'blk', axis=0, tiled=True)]
    all_to_all x0 -> x1, waiting for transfers between devices: none -> 46.9 us  [resolve_state(): value_now = lax.all_to_all(reached, peer_axis, 0, 0)]
    all_to_all x0 -> x1, starting transfers between devices: none -> 17.4 us  [resolve_state(): value_now = lax.all_to_all(reached, peer_axis, 0, 0)]
    another operation x0 -> x1, local copies, waits for them, and re-layouts: none -> 2.72 us  [resolve_state(): reached = jnp.stack([sample] * lax.psum(1, peer_axis))]
    reduce_scatter x1, waiting for transfers between devices: 48.5 us -> 50.9 us  [local(): summed = lax.psum_scatter(terms, 'mpo', scatter_dimension=2, tiled=True)]
  transfers between devices with their start and end apart: 2 -> 2, of which waited for: 2 -> 2; matrix products, arithmetic and copies ran while one was open for 2% -> 1% of each run, Pallas kernels for 0% -> 0%
where the time goes in v1:
time: 147 us
  waiting for transfers between devices  97.8 us (67%)
  starting transfers between devices  17.4 us (12%)
  between operations  13.5 us (9%)
  local copies, waits for them, and re-layouts  8.31 us (6%)
  matrix products  7.77 us (5%)
  other arithmetic  1.97 us (1%)
    reduce_scatter x1, waiting for transfers between devices, local(): summed = lax.psum_scatter(terms, 'mpo', scatter_dimension=2, tiled=True)  50.9 us
    all_to_all x1, waiting for transfers between devices, resolve_state(): value_now = lax.all_to_all(reached, peer_axis, 0, 0)  46.9 us
    all_to_all x1, starting transfers between devices, resolve_state(): value_now = lax.all_to_all(reached, peer_axis, 0, 0)  17.4 us
    dot_general x1, matrix products, local(): jnp.einsum('bik,bjk->bij', left, picked, preferred_element_type=jnp.float32)  7.77 us
    gather x1, local copies, waits for them, and re-layouts, local(): picked = jnp.take(every_right, places, axis=0)  4.35 us
  transfers between devices with their start and end apart: 2, of which 2 were waited for; matrix products, arithmetic and copies ran while one was open for 1% of the time, Pallas kernels for 0%

profile of v1, /device:TPU:1, one launch (start us, length us, event | category | flops | bytes accessed | tf_op | source)
XLA Modules:
  0.0 146.8 jit_solution(1059834565302476337)
XLA Ops:
  6.5 0.0 copy-start
  6.5 0.0 copy-start.2
  6.5 0.0 copy-start.1
  6.5 2.7 %stack.3 = bf16[64,1,128,128]{3,2,1,0:T(8,128)(2,1)} broadcast(bf16[128,128]{1,0:T(8,128)(2,1)} %bitcast.14), dimensions={2,3} | broadcast | bytes 2129920 | tf_op jit(solution)/shard_map/stack | solution.py:10
  9.3 17.4 %all-to-all-start = ((bf16[64,1,128,128]{3,2,1,0:T(8,128)(2,1)}), bf16[64,1,128,128]{3,2,1,0:T(8,128)(2,1)}, u32[]{:S(2)}, u32[]{:S(2)}) async-start(bf16[64,1,128,128]{3,2,1,0:T(8,128)(2,1)} %stack.3), calls=%async_computation | async-start | bytes 4194304 | tf_op jit(solution)/shard_map/all_to_all | solution.py:11
  26.7 0.0 reduce-scatter.2.cloned.1.call-start
  26.7 0.0 copy-done.2
  26.7 0.0 copy-done.1
  26.8 1.2 gather_fusion
  28.0 46.9 %all-to-all-done = bf16[64,1,128,128]{3,2,1,0:T(8,128)(2,1)} async-done(((bf16[64,1,128,128]{3,2,1,0:T(8,128)(2,1)}), bf16[64,1,128,128]{3,2,1,0:T(8,128)(2,1)}, u32[]{:S(2)}, u32[]{:S(2)}) %all-to-all-start) | async-done | bytes 2097184 | tf_op jit(solution)/shard_map/all_to_all | solution.py:11
  75.0 0.0 copy-start.3
  75.0 4.3 %gather_fusion.1 = bf16[96,128,128]{2,1,0:T(8,128)(2,1)} fusion(bf16[64,128,128]{2,1,0:T(8,128)(2,1)} %bitcast.5, s32[1024]{0:T(1024)S(1)} %pad_clamp_fusion), kind=kCustom, calls=%fused_computation.1 | custom fusion | bytes 6291840 | tf_op jit(solution)/shard_map/jit(_take)/gather | solution.py:24
  79.3 0.0 copy-done
  79.3 0.0 copy-done.3
  79.3 7.8 %fusion = f32[96,128,128]{1,2,0:T(8,128)} fusion(bf16[96,128,128]{2,1,0:T(8,128)(2,1)} %gather_fusion.1, pred[96]{0:T(512)(128)(4,1)S(1)} %get-tuple-element.5, bf16[96,128,128]{2,1,0:T(8,128)(2,1)S(1)} %copy-done, pred[96]{0:T(512)(128)(4,1)S(1)} %compare_and_fusion, bf16[128,128]{1,0:T(8,128)(2,1)S(1)} %bitcast.16), kind=kOutput, calls=%fused_computation.2 | convolution fusion | flops 810024960 | bytes 12615872 | tf_op jit(solution)/shard_map/bik,bjk->bij/dot_general | solution.py:25
  87.1 0.0 reduce-scatter.2.cloned.1.call-update
  87.1 50.9 %reduce-scatter.2.cloned.1.call-done = f32[96,128,16]{1,2,0:T(8,128)} async-done(((f32[96,128,128]{1,2,0:T(8,128)}), f32[96,128,16]{1,2,0:T(8,128)}) %reduce-scatter.2.cloned.1.call-update) | async-done | bytes 786448 | tf_op jit(solution)/shard_map/reduce_scatter | solution.py:26
  138.0 1.9 %convert_element_type.7 = bf16[96,128,16]{1,2,0:T(8,128)(2,1)} convert(f32[96,128,16]{1,2,0:T(8,128)} %reduce-scatter.2.cloned.1.call-done) | non-fusion elementwise | flops 196608 | bytes 1179648 | tf_op jit(solution)/shard_map/convert_element_type | solution.py:27
  (5 shorter events, 0.0 us)
Async XLA Ops:
  6.5 72.8 %copy-start = (bf16[96,128,128]{2,1,0:T(8,128)(2,1)S(1)}, bf16[96,128,128]{2,1,0:T(8,128)(2,1)}, u32[]{:S(2)}) copy-start(bf16[96,128,128]{2,1,0:T(8,128)(2,1)} %param.5) | copy-start | bytes 9437188
  6.5 20.2 %copy-start.2 = (s32[96,1]{0,1:T(1,128)S(1)}, s32[96,1]{0,1:T(1,128)}, u32[]{:S(2)}) copy-start(s32[96,1]{0,1:T(1,128)} %param.8) | copy-start | bytes 1156
  6.5 20.2 %copy-start.1 = (s32[64]{0:T(128)S(1)}, s32[64]{0:T(128)}, u32[]{:S(2)}) copy-start(s32[64]{0:T(128)} %param.9) | copy-start | bytes 772
  9.3 65.7 %all-to-all-start = ((bf16[64,1,128,128]{3,2,1,0:T(8,128)(2,1)}), bf16[64,1,128,128]{3,2,1,0:T(8,128)(2,1)}, u32[]{:S(2)}, u32[]{:S(2)}) async-start(bf16[64,1,128,128]{3,2,1,0:T(8,128)(2,1)} %stack.3), calls=%async_computation | async-start | bytes 4194304 | tf_op jit(solution)/shard_map/all_to_all | solution.py:11
  26.7 111.3 %reduce-scatter.2.cloned.1.call-start = ((), (), s32[]{:S(2)}) async-start(), calls=%async_computation.2 | async-start | bytes 7077888 | tf_op jit(solution)/shard_map/reduce_scatter | solution.py:26
  75.0 4.4 %copy-start.3 = (bf16[1,1,128,128]{3,2,1,0:T(8,128)(2,1)S(1)}, bf16[1,1,128,128]{3,2,1,0:T(8,128)(2,1)}, u32[]{:S(2)}) copy-start(bf16[1,1,128,128]{3,2,1,0:T(8,128)(2,1)} %param.6) | copy-start | bytes 98308
Sparse Core Ops, SparseCore 0:
  87.2 50.7 reduce-scatter.1
